TPU v7x, 256 devices: a whole 4x4x8 slice. The times are simulated.
256 devices in a mesh: dp: 8 (over x, core), expert: 32 (over y, z).
Axes of the slice: x: 4, y: 4, z: 8, core: 2. Of those that a mesh axis runs over, the one named last changes fastest.
Arguments:
- tokens: bfloat16 [8192, 2048], P(('dp', 'expert')), may hold values from -6 to 6
- expert_ids: int32 [8192, 8], P(('dp', 'expert')), may hold values from 0 to 31, all different within a row; in each aligned block of 32 rows (0 to 31, 32 to 63, ...) at most 16 rows name the same one
- gate_weights: float32 [8192, 8], P(('dp', 'expert')), may hold values from 0.05 to 0.35
- grad_output: bfloat16 [8192, 2048], P(('dp', 'expert')), may hold values from -6 to 6
- w_gate_up: bfloat16 [32, 2048, 1536], P('expert'), may hold values from -0.125 to 0.125
- w_down: bfloat16 [32, 768, 2048], P('expert'), may hold values from -0.21875 to 0.21875
Outputs:
- mixed: bfloat16 [8192, 2048], P(('dp', 'expert'))
- grad_tokens: bfloat16 [8192, 2048], P(('dp', 'expert'))
- grad_gates: float32 [8192, 8], P(('dp', 'expert'))
- grad_gate_up: float32 [32, 2048, 1536], P('expert', 'dp')
- grad_down: float32 [32, 768, 2048], P('expert', None, 'dp')
Inputs may be any that keep to these rules, and one draw needn't show every extreme that they name: `expert_ids`: in each block of 32 rows (the rows of one device) every expert is named at most 16 times, a bound that some block reaches; a row names 8 different experts, and every expert is named somewhere.
All inputs are finite; a program needn't handle non-finite values.
Results may differ from a plain program's by a relative error of at most 0.015.
Values may be sent and summed in bfloat16 or wider, within the bound.
No kernel may reach another device: no remote copies, remote signals or barrier semaphores. Data moves between devices by JAX's collectives and lax.ppermute only.
A program may use at most 128 MiB of HBM per device.

v0:
```python
import jax
import jax.numpy as jnp
from jax import lax
from jax.sharding import PartitionSpec as P


def swish_parts(gate_up, hidden_units):
    gate_half = gate_up[..., :hidden_units]
    up_half = gate_up[..., hidden_units:]
    sigmoid_part = jax.nn.sigmoid(gate_half)
    return (gate_half, up_half, sigmoid_part)


def expert_forward(stacked, w_gate_up, w_down, hidden_units):
    gate_up = jnp.einsum("sjmd,jdf->sjmf", stacked, w_gate_up, preferred_element_type=jnp.float32)
    gate_half, up_half, sigmoid_part = swish_parts(gate_up, hidden_units)
    hidden = (gate_half * sigmoid_part * up_half).astype(jnp.bfloat16)
    out_rows = jnp.einsum(
        "sjmf,jfd->sjmd", hidden, w_down, preferred_element_type=jnp.float32
    ).astype(jnp.bfloat16)
    return (gate_up, out_rows)


def expert_backward(gate_up, grad_rows, w_gate_up, w_down, hidden_units):
    gate_half, up_half, sigmoid_part = swish_parts(gate_up, hidden_units)
    swish = gate_half * sigmoid_part
    hidden = (swish * up_half).astype(jnp.bfloat16)
    grad_hidden = jnp.einsum(
        "sjmd,jfd->sjmf", grad_rows, w_down, preferred_element_type=jnp.float32
    )
    grad_gate = grad_hidden * up_half * sigmoid_part * (1.0 + gate_half * (1.0 - sigmoid_part))
    grad_up = grad_hidden * swish
    grad_act = jnp.concatenate([grad_gate, grad_up], axis=3).astype(jnp.bfloat16)
    grad_in = jnp.einsum(
        "sjmf,jdf->sjmd", grad_act, w_gate_up, preferred_element_type=jnp.float32
    ).astype(jnp.bfloat16)
    return (hidden, grad_act, grad_in)


def weight_sums(stacked_x, grad_act, hidden, grad_rows):
    down_local = jnp.einsum("sjmf,sjmd->jfd", hidden, grad_rows, preferred_element_type=jnp.float32)
    gate_up_local = jnp.einsum(
        "sjmd,sjmf->jdf", stacked_x, grad_act, preferred_element_type=jnp.float32
    )
    grad_gate_up, grad_down = (
        lax.psum_scatter(
            gate_up_local.astype(jnp.bfloat16), "dp", scatter_dimension=1, tiled=True
        ).astype(jnp.float32),
        lax.psum_scatter(
            down_local.astype(jnp.bfloat16), "dp", scatter_dimension=2, tiled=True
        ).astype(jnp.float32),
    )
    return (grad_gate_up, grad_down)


def body(tokens, expert_ids, gate_weights, grad_output, w_gate_up, w_down):
    token_count, top_count = expert_ids.shape
    width = tokens.shape[1]
    per_device = w_gate_up.shape[0]
    hidden_units = w_down.shape[1]
    owners = lax.axis_size("expert")
    expert_total = owners * per_device
    capacity = min(token_count, 2 * token_count * top_count // expert_total)
    pair_count = token_count * top_count
    buffer_rows = expert_total * capacity
    flat_ids = expert_ids.reshape(-1)
    onehot = flat_ids[:, None] == jnp.arange(expert_total, dtype=jnp.int32)[None, :]
    pair_axis = jnp.arange(pair_count, dtype=jnp.int32)
    lower = (pair_axis[:, None] > pair_axis[None, :]).astype(jnp.bfloat16)
    before = jnp.dot(lower, onehot.astype(jnp.bfloat16), preferred_element_type=jnp.float32)
    slots = jnp.sum(jnp.where(onehot, before, 0.0), axis=1).astype(jnp.int32)
    target = flat_ids * capacity + slots
    select = target[:, None] == jnp.arange(buffer_rows, dtype=jnp.int32)[None, :]
    select_f = select.astype(jnp.float32)
    placing = jnp.sum(
        select.reshape(token_count, top_count, buffer_rows).astype(jnp.bfloat16), axis=1
    )
    place_rows = placing.T
    row_gate = jnp.sum(select_f * gate_weights.reshape(-1)[:, None], axis=0)
    outgoing = (
        jnp.dot(place_rows, tokens, preferred_element_type=jnp.float32)
        .astype(jnp.bfloat16)
        .reshape(expert_total, capacity, width)
    )
    routed_grad = jnp.dot(place_rows, grad_output, preferred_element_type=jnp.float32)
    grad_buffer = (
        (row_gate[:, None] * routed_grad)
        .astype(jnp.bfloat16)
        .reshape(expert_total, capacity, width)
    )
    received = lax.all_to_all(outgoing, "expert", split_axis=0, concat_axis=0, tiled=True)
    stacked = received.reshape(owners, per_device, received.shape[1], width)
    gate_up_here, out_rows = expert_forward(stacked, w_gate_up, w_down, hidden_units)
    returned = out_rows.reshape(received.shape)
    kept_gate_up = gate_up_here.reshape(received.shape[0], received.shape[1], 2 * hidden_units)
    stacked_x = received.reshape(owners, per_device, capacity, width)
    gate_up = kept_gate_up.reshape(owners, per_device, capacity, 2 * hidden_units)
    back = lax.all_to_all(returned, "expert", split_axis=0, concat_axis=0, tiled=True)
    grad_arrived = lax.all_to_all(grad_buffer, "expert", split_axis=0, concat_axis=0, tiled=True)
    grad_rows = grad_arrived.reshape(owners, per_device, capacity, width)
    hidden, grad_act, grad_in = expert_backward(gate_up, grad_rows, w_gate_up, w_down, hidden_units)
    grad_back = lax.all_to_all(
        grad_in.reshape(expert_total, capacity, width),
        "expert",
        split_axis=0,
        concat_axis=0,
        tiled=True,
    )
    back_rows = back.reshape(buffer_rows, width).astype(jnp.float32)
    weighted_back = row_gate[:, None] * back_rows
    mixed = jnp.dot(
        placing.astype(jnp.float32),
        weighted_back,
        precision=lax.Precision.HIGHEST,
        preferred_element_type=jnp.float32,
    ).astype(jnp.bfloat16)
    row_inner = jnp.sum(back_rows * routed_grad, axis=1)
    grad_gates = jnp.sum(select_f * row_inner[None, :], axis=1).reshape(token_count, top_count)
    grad_tokens = jnp.dot(
        placing, grad_back.reshape(buffer_rows, width), preferred_element_type=jnp.float32
    ).astype(jnp.bfloat16)
    grad_gate_up, grad_down = weight_sums(stacked_x, grad_act, hidden, grad_rows)
    return (mixed, grad_tokens, grad_gates, grad_gate_up, grad_down)


def solution(mesh):
    in_specs = (
        P(("dp", "expert"), None),
        P(("dp", "expert"), None),
        P(("dp", "expert"), None),
        P(("dp", "expert"), None),
        P("expert", None, None),
        P("expert", None, None),
    )
    out_specs = (
        P(("dp", "expert"), None),
        P(("dp", "expert"), None),
        P(("dp", "expert"), None),
        P("expert", "dp", None),
        P("expert", None, "dp"),
    )
    return jax.shard_map(body, mesh=mesh, in_specs=in_specs, out_specs=out_specs, check_vma=False)
```

profile of v0, /device:TPU:2, one launch (start us, length us, event | category | flops | bytes accessed | tf_op | source)
XLA Modules:
  0.0 291.5 jit_solution(11906623702706875263)
XLA Ops:
  7.2 0.9 copy.24
  8.2 0.2 fusion.28
  8.5 0.2 fusion.33
  8.8 1.8 convolution_convert_fusion
  10.5 62.6 %all_to_all.20 = bf16[32,16,2048]{2,1,0:T(8,128)(2,1)S(1)} all-to-all(bf16[32,16,2048]{2,1,0:T(8,128)(2,1)S(1)} %bitcast.83), channel_id=1, replica_groups=mesh['dp'=8,'expert'=32] {'expert'}, dimensions={0} | all-to-all | bytes 4194304 | tf_op jit(solution)/shard_map/all_to_all | solution.py:91
  73.1 3.4 %fusion.7 = f32[32,1,16,1536]{3,2,0,1:T(8,128)S(1)} fusion(bf16[32,16,2048]{2,1,0:T(8,128)(2,1)S(1)} %all_to_all.20, bf16[1,2048,1536]{2,1,0:T(8,128)(2,1)S(1)} %copy-done.9), kind=kOutput, calls=%fused_computation.12 | convolution fusion | flops 3221225472 | bytes 11534336 | tf_op jit(solution)/shard_map/sjmd,jdf->sjmf/dot_general | solution.py:15
  76.6 1.6 copy-done.1
  78.2 0.5 fusion.29
  78.7 0.9 copy-done.5
  79.6 3.2 %fusion.14 = bf16[32,16,2048]{2,1,0:T(8,128)(2,1)} fusion(bf16[32,16,768]{2,1,0:T(8,128)(2,1)S(1)} %fusion.29, bf16[1,768,2048]{2,1,0:T(8,128)(2,1)S(1)} %copy-done), kind=kOutput, calls=%fused_computation.17 | convolution fusion | flops 1611661312 | bytes 6029312 | tf_op jit(solution)/shard_map/sjmf,jfd->sjmd/dot_general | solution.py:18
  82.8 5.3 %all-to-all-start.1 = ((bf16[32,16,2048]{2,1,0:T(8,128)(2,1)}), bf16[32,16,2048]{2,1,0:T(8,128)(2,1)}, u32[]{:S(2)}, u32[]{:S(2)}) async-start(bf16[32,16,2048]{2,1,0:T(8,128)(2,1)} %fusion.14), calls=%async_computation.1 | async-start | bytes 4194304 | tf_op jit(solution)/shard_map/all_to_all | solution.py:98
  88.3 49.4 %all-to-all-done.1 = bf16[32,16,2048]{2,1,0:T(8,128)(2,1)} async-done(((bf16[32,16,2048]{2,1,0:T(8,128)(2,1)}), bf16[32,16,2048]{2,1,0:T(8,128)(2,1)}, u32[]{:S(2)}, u32[]{:S(2)}) %all-to-all-start.1) | async-done | bytes 2097184 | tf_op jit(solution)/shard_map/all_to_all | solution.py:98
  137.7 2.4 fusion.6
  140.1 0.3 select_reduce_fusion
  140.4 0.3 multiply_convert_fusion
  140.7 56.7 %all_to_all.21 = bf16[32,16,2048]{2,1,0:T(8,128)(2,1)S(1)} all-to-all(bf16[32,16,2048]{2,1,0:T(8,128)(2,1)S(1)} %bitcast.82), channel_id=1, replica_groups=mesh['dp'=8,'expert'=32] {'expert'}, dimensions={0} | all-to-all | bytes 4194304 | tf_op jit(solution)/shard_map/all_to_all | solution.py:99
  197.4 1.4 copy-done.4
  198.8 3.5 %fusion.20 = bf16[1,768,2048]{2,1,0:T(8,128)(2,1)} fusion(bf16[32,16,768]{2,1,0:T(8,128)(2,1)S(1)} %copy-done.6, bf16[32,16,2048]{2,1,0:T(8,128)(2,1)S(1)} %all_to_all.21), kind=kOutput, calls=%fused_computation.20 | convolution fusion | flops 1612185600 | bytes 6029312 | tf_op jit(solution)/shard_map/sjmf,sjmd->jfd/dot_general | solution.py:41
  202.3 0.2 reduce-scatter.3.cloned.1.call-start
  202.6 4.9 %fusion.31 = (bf16[32,16,768]{2,1,0:T(8,128)(2,1)S(1)}, bf16[32,16,768]{2,1,0:T(8,128)(2,1)S(1)}) fusion(f32[32,1,16,1536]{3,2,0,1:T(8,128)} %copy-done.1, bf16[32,16,2048]{2,1,0:T(8,128)(2,1)} %copy-done.4, bf16[1,768,2048]{2,1,0:T(8,128)(2,1)S(1)} %copy-done), kind=kOutput, calls=%fused_computation.38 | convolution fusion | flops 1615724544 | bytes 9961472 | tf_op jit(solution)/shard_map/sjmd,jfd->sjmf/dot_general | solution.py:28
  207.5 0.9 copy-done.10
  208.3 0.3 copy-done.11
  208.6 5.6 %fusion = bf16[1,2048,1536]{2,1,0:T(8,128)(2,1)} fusion(bf16[32,16,2048]{2,1,0:T(8,128)(2,1)S(1)} %copy-done.3, bf16[32,16,768]{2,1,0:T(8,128)(2,1)S(1)} %get-tuple-element.18, bf16[32,16,768]{2,1,0:T(8,128)(2,1)S(1)} %get-tuple-element.17), kind=kOutput, calls=%fused_computation.1 | convolution fusion | flops 3227516928 | bytes 9961472 | tf_op jit(solution)/shard_map/sjmd,sjmf->jdf/dot_general | solution.py:42
  214.3 8.1 %fusion.17 = bf16[32,16,2048]{2,1,0:T(8,128)(2,1)} fusion(bf16[1,2048,1536]{2,1,0:T(8,128)(2,1)} %param.10, bf16[32,16,768]{2,1,0:T(8,128)(2,1)} %copy-done.11, bf16[32,16,768]{2,1,0:T(8,128)(2,1)} %copy-done.10), kind=kOutput, calls=%fused_computation.18 | convolution fusion | flops 3225419776 | bytes 9961472 | tf_op jit(solution)/shard_map/sjmf,jdf->sjmd/dot_general | solution.py:34
  222.4 5.1 %all-to-all-start.3 = ((bf16[32,16,2048]{2,1,0:T(8,128)(2,1)}), bf16[32,16,2048]{2,1,0:T(8,128)(2,1)}, u32[]{:S(2)}, u32[]{:S(2)}) async-start(bf16[32,16,2048]{2,1,0:T(8,128)(2,1)} %fusion.17), calls=%async_computation.3 | async-start | bytes 4194304 | tf_op jit(solution)/shard_map/all_to_all | solution.py:102
  227.6 0.7 copy.27
  228.2 4.2 %fusion.21 = bf16[32,2048]{1,0:T(8,128)(2,1)} fusion(bf16[32,512]{1,0:T(8,128)(2,1)S(1)} %fusion.33, bf16[512,2048]{1,0:T(8,128)(2,1)} %bitcast.21, f32[512]{0:T(512)S(1)} %get-tuple-element.16), kind=kOutput, calls=%fused_computation.21 | convolution fusion | flops 404815872 | bytes 2263040 | tf_op jit(solution)/shard_map/dot_general | solution.py:111
  232.5 44.6 %all-to-all-done.3 = bf16[32,16,2048]{2,1,0:T(8,128)(2,1)} async-done(((bf16[32,16,2048]{2,1,0:T(8,128)(2,1)}), bf16[32,16,2048]{2,1,0:T(8,128)(2,1)}, u32[]{:S(2)}, u32[]{:S(2)}) %all-to-all-start.3) | async-done | bytes 2097184 | tf_op jit(solution)/shard_map/all_to_all | solution.py:102
  277.1 2.7 convolution_convert_fusion.1
  279.9 1.9 convert_element_type.94
  281.8 0.4 reduce-scatter.3.cloned.1.call-done
  282.2 2.5 convert_element_type.91
  (31 shorter events, 0.6 us)
Async XLA Ops:
  7.2 72.4 %copy-start = (bf16[1,768,2048]{2,1,0:T(8,128)(2,1)S(1)}, bf16[1,768,2048]{2,1,0:T(8,128)(2,1)}, u32[]{:S(2)}) copy-start(bf16[1,768,2048]{2,1,0:T(8,128)(2,1)} %param.11) | copy-start | bytes 9437188
  8.7 64.4 %copy-start.9 = (bf16[1,2048,1536]{2,1,0:T(8,128)(2,1)S(1)}, bf16[1,2048,1536]{2,1,0:T(8,128)(2,1)}, u32[]{:S(2)}) copy-start(bf16[1,2048,1536]{2,1,0:T(8,128)(2,1)} %param.10) | copy-start | bytes 18874372
  73.1 3.4 %copy-start.2 = (bf16[32,16,2048]{2,1,0:T(8,128)(2,1)}, bf16[32,16,2048]{2,1,0:T(8,128)(2,1)S(1)}, u32[]{:S(2)}) copy-start(bf16[32,16,2048]{2,1,0:T(8,128)(2,1)S(1)} %all_to_all.20) | copy-start | bytes 6291460
  76.6 1.6 copy-start.1
  78.7 0.9 copy-start.5
  82.8 5.3 %copy-start.8 = (f32[32,8]{0,1:T(8,128)S(1)}, f32[32,8]{0,1:T(8,128)}, u32[]{:S(2)}) copy-start(f32[32,8]{0,1:T(8,128)} %param.8) | copy-start | bytes 3076
  82.8 54.9 %copy-start.7 = (bf16[32,2048]{1,0:T(8,128)(2,1)S(1)}, bf16[32,2048]{1,0:T(8,128)(2,1)}, u32[]{:S(2)}) copy-start(bf16[32,2048]{1,0:T(8,128)(2,1)} %param.9) | copy-start | bytes 393220
  82.8 54.9 %all-to-all-start.1 = ((bf16[32,16,2048]{2,1,0:T(8,128)(2,1)}), bf16[32,16,2048]{2,1,0:T(8,128)(2,1)}, u32[]{:S(2)}, u32[]{:S(2)}) async-start(bf16[32,16,2048]{2,1,0:T(8,128)(2,1)} %fusion.14), calls=%async_computation.1 | async-start | bytes 4194304 | tf_op jit(solution)/shard_map/all_to_all | solution.py:98
  88.1 191.8 %reduce-scatter.5.cloned.1.call-start = ((), (), s32[]{:S(2)}) async-start(), calls=%async_computation.7 | async-start | bytes 3538944 | tf_op jit(solution)/shard_map/reduce_scatter | solution.py:49
  140.7 58.1 %copy-start.6 = (bf16[32,16,768]{2,1,0:T(8,128)(2,1)S(1)}, bf16[32,16,768]{2,1,0:T(8,128)(2,1)}, u32[]{:S(2)}) copy-start(bf16[32,16,768]{2,1,0:T(8,128)(2,1)} %copy-done.5) | copy-start | bytes 2359300
  197.4 1.4 copy-start.4
  202.3 79.9 %reduce-scatter.3.cloned.1.call-start = ((), (), s32[]{:S(2)}) async-start(), calls=%async_computation.6 | async-start | bytes 7077888 | tf_op jit(solution)/shard_map/reduce_scatter | solution.py:46
  202.6 6.0 %copy-start.3 = (bf16[32,16,2048]{2,1,0:T(8,128)(2,1)S(1)}, bf16[32,16,2048]{2,1,0:T(8,128)(2,1)}, u32[]{:S(2)}) copy-start(bf16[32,16,2048]{2,1,0:T(8,128)(2,1)} %copy-done.2) | copy-start | bytes 6291460
  207.5 0.9 copy-start.10
  207.5 1.1 copy-start.11
  222.4 54.8 %all-to-all-start.3 = ((bf16[32,16,2048]{2,1,0:T(8,128)(2,1)}), bf16[32,16,2048]{2,1,0:T(8,128)(2,1)}, u32[]{:S(2)}, u32[]{:S(2)}) async-start(bf16[32,16,2048]{2,1,0:T(8,128)(2,1)} %fusion.17), calls=%async_computation.3 | async-start | bytes 4194304 | tf_op jit(solution)/shard_map/all_to_all | solution.py:102
Sparse Core Ops, SparseCore 0:
  202.5 31.5 reduce-scatter.4
  236.6 45.6 reduce-scatter.2
where the time goes:
time: 295 us; the launch traced here: 292 us
  blocking collectives  119 us (40%)
  waiting for transfers between devices  94.5 us (32%)
  matrix products  40.1 us (14%)
  between operations  14.2 us (5%)
  starting transfers between devices  10.7 us (4%)
  local copies, waits for them, and re-layouts  7.08 us (2%)
  other arithmetic  5.67 us (2%)
    all_to_all x1, blocking collectives, body(): lax.all_to_all(outgoing, 'expert', split_axis=0, concat_axis=0, tiled=True)  62.6 us
    all_to_all x1, blocking collectives, body(): lax.all_to_all(grad_buffer, 'expert', split_axis=0, concat_axis=0, tiled=...  56.7 us
    all_to_all x1, waiting for transfers between devices, body(): lax.all_to_all(returned, 'expert', split_axis=0, concat_axis=0, tiled=True)  49.4 us
    all_to_all x1, waiting for transfers between devices, body(): lax.all_to_all(grad_in.reshape(expert_total, capacity, width), 'expert',...  44.6 us
    dot_general x1, matrix products, expert_backward(): jnp.einsum('sjmf,jdf->sjmd', grad_act, w_gate_up, preferred_element_type=...  8.1 us
    unnamed x27, local copies, waits for them, and re-layouts  6.75 us
  transfers between devices with their start and end apart: 4, of which 3 were waited for; matrix products, arithmetic and copies ran while one was open for 10% of the time, Pallas kernels for 0%

commit v1 on v0

v1 whole, which is shorter than its diff:
```python
import jax
import jax.numpy as jnp
from jax import lax
from jax.sharding import PartitionSpec as P


def swish_parts(gate_up, hidden_units):
    gate_half = gate_up[..., :hidden_units]
    up_half = gate_up[..., hidden_units:]
    sigmoid_part = jax.nn.sigmoid(gate_half)
    return (gate_half, up_half, sigmoid_part)


def body(tokens, expert_ids, gate_weights, grad_output, w_gate_up, w_down):
    token_count, top_count = expert_ids.shape
    width = tokens.shape[1]
    per_device = w_gate_up.shape[0]
    hidden_units = w_down.shape[1]
    owners = lax.axis_size("expert")
    expert_total = owners * per_device
    capacity = min(token_count, 2 * token_count * top_count // expert_total)
    pair_count = token_count * top_count
    me = lax.axis_index("expert")

    all_tokens = lax.all_gather(tokens, "expert", tiled=True).reshape(owners, token_count, width)
    all_ids = lax.all_gather(expert_ids, "expert", tiled=True).reshape(owners, pair_count)
    all_gates = lax.all_gather(gate_weights, "expert", tiled=True).reshape(owners, pair_count)
    all_grad = lax.all_gather(grad_output, "expert", tiled=True).reshape(owners, token_count, width)

    local_experts = me * per_device + jnp.arange(per_device, dtype=jnp.int32)
    onehot = all_ids[:, :, None] == local_experts[None, None, :]
    onehot_i = onehot.astype(jnp.int32)
    slots = jnp.cumsum(onehot_i, axis=1) - onehot_i
    slot_axis = jnp.arange(capacity, dtype=jnp.int32)
    sel = jnp.logical_and(onehot[..., None], slots[..., None] == slot_axis).transpose(2, 0, 3, 1)
    sel_f = sel.astype(jnp.float32)
    row_gate = jnp.sum(sel_f * all_gates[None, :, None, :], axis=3)
    sel_tok = jnp.sum(
        sel.reshape(per_device, owners, capacity, token_count, top_count).astype(jnp.bfloat16),
        axis=4,
    )

    x_rows = jnp.einsum(
        "jsct,std->jscd", sel_tok, all_tokens, preferred_element_type=jnp.float32
    ).astype(jnp.bfloat16)
    dy_rows = jnp.einsum(
        "jsct,std->jscd", sel_tok, all_grad, preferred_element_type=jnp.float32
    )
    x_rows = x_rows.reshape(per_device, owners * capacity, width)
    dy_rows = dy_rows.reshape(per_device, owners * capacity, width)
    row_gate = row_gate.reshape(per_device, owners * capacity)

    gate_up = jnp.einsum("jrd,jdf->jrf", x_rows, w_gate_up, preferred_element_type=jnp.float32)
    gate_half, up_half, sigmoid_part = swish_parts(gate_up, hidden_units)
    swish = gate_half * sigmoid_part
    hidden = (swish * up_half).astype(jnp.bfloat16)
    out_rows = jnp.einsum(
        "jrf,jfd->jrd", hidden, w_down, preferred_element_type=jnp.float32
    ).astype(jnp.bfloat16)

    grad_rows = (row_gate[..., None] * dy_rows).astype(jnp.bfloat16)
    grad_hidden = jnp.einsum("jrd,jfd->jrf", grad_rows, w_down, preferred_element_type=jnp.float32)
    grad_gate = grad_hidden * up_half * sigmoid_part * (1.0 + gate_half * (1.0 - sigmoid_part))
    grad_up = grad_hidden * swish
    grad_act = jnp.concatenate([grad_gate, grad_up], axis=2).astype(jnp.bfloat16)
    grad_in = jnp.einsum(
        "jrf,jdf->jrd", grad_act, w_gate_up, preferred_element_type=jnp.float32
    ).astype(jnp.bfloat16)

    out_f = out_rows.astype(jnp.float32)
    row_inner = jnp.sum(out_f * dy_rows, axis=2).reshape(per_device, owners, capacity)
    gate_part = jnp.sum(sel_f * row_inner[..., None], axis=(0, 2)).reshape(owners * token_count, top_count)
    weighted = (row_gate[..., None] * out_f).astype(jnp.bfloat16)
    mixed_part = jnp.einsum(
        "jsct,jscd->std",
        sel_tok,
        weighted.reshape(per_device, owners, capacity, width),
        preferred_element_type=jnp.float32,
    ).astype(jnp.bfloat16)
    mixed = lax.psum_scatter(
        mixed_part.reshape(owners * token_count, width), "expert", scatter_dimension=0, tiled=True
    )
    grad_gates = lax.psum_scatter(gate_part, "expert", scatter_dimension=0, tiled=True)
    tokens_part = jnp.einsum(
        "jsct,jscd->std",
        sel_tok,
        grad_in.reshape(per_device, owners, capacity, width),
        preferred_element_type=jnp.float32,
    ).astype(jnp.bfloat16)
    grad_tokens = lax.psum_scatter(
        tokens_part.reshape(owners * token_count, width), "expert", scatter_dimension=0, tiled=True
    )

    down_local = jnp.einsum("jrf,jrd->jfd", hidden, grad_rows, preferred_element_type=jnp.float32)
    gate_up_local = jnp.einsum("jrd,jrf->jdf", x_rows, grad_act, preferred_element_type=jnp.float32)
    grad_gate_up = lax.psum_scatter(
        gate_up_local.astype(jnp.bfloat16), "dp", scatter_dimension=1, tiled=True
    ).astype(jnp.float32)
    grad_down = lax.psum_scatter(
        down_local.astype(jnp.bfloat16), "dp", scatter_dimension=2, tiled=True
    ).astype(jnp.float32)
    return (mixed, grad_tokens, grad_gates, grad_gate_up, grad_down)


def solution(mesh):
    in_specs = (
        P(("dp", "expert"), None),
        P(("dp", "expert"), None),
        P(("dp", "expert"), None),
        P(("dp", "expert"), None),
        P("expert", None, None),
        P("expert", None, None),
    )
    out_specs = (
        P(("dp", "expert"), None),
        P(("dp", "expert"), None),
        P(("dp", "expert"), None),
        P("expert", "dp", None),
        P("expert", None, "dp"),
    )
    return jax.shard_map(body, mesh=mesh, in_specs=in_specs, out_specs=out_specs, check_vma=False)
```

time: 295 us -> 954 us (3.23)
  waiting for transfers between devices: 94.5 us -> 784 us
  blocking collectives: 119 us -> 89.2 us
  starting transfers between devices: 10.7 us -> 0.46 us
    reduce_scatter x2 -> x5, waiting for transfers between devices: 0.43 us -> 713 us  [the longest x1 227 us: body(): lax.psum_scatter(mixed_part.reshape(owners * token_count, width), 'expert...]
    all_to_all x2 -> x0, blocking collectives: 119 us -> none  [the longest x1 62.6 us: body(): lax.all_to_all(outgoing, 'expert', split_axis=0, concat_axis=0, tiled=True)]
    all_to_all x2 -> x0, waiting for transfers between devices: 94 us -> none  [the longest x1 49.4 us: body(): lax.all_to_all(returned, 'expert', split_axis=0, concat_axis=0, tiled=True)]
    all_gather x0 -> x2, blocking collectives: none -> 89.2 us  [the longest x1 46.8 us: body(): lax.all_gather(expert_ids, 'expert', tiled=True).reshape(owners, pair_count)]
    all_gather x0 -> x2, waiting for transfers between devices: none -> 69.6 us  [the longest x1 69.6 us: body(): lax.all_gather(grad_output, 'expert', tiled=True)]
    all_to_all x2 -> x0, starting transfers between devices: 10.4 us -> none  [the longest x1 5.29 us: body(): lax.all_to_all(returned, 'expert', split_axis=0, concat_axis=0, tiled=True)]
    dot_general x11 -> x10, matrix products: 40.1 us -> 47.9 us  [the longest x1 7.05 us: body(): jnp.einsum('jrd,jdf->jrf', x_rows, w_gate_up, preferred_element_type=jnp....]
  transfers between devices with their start and end apart: 4 -> 7, of which waited for: 3 -> 6; matrix products, arithmetic and copies ran while one was open for 10% -> 5% of each run, Pallas kernels for 0% -> 0%
where the time goes in v1:
time: 954 us; the launch traced here: 953 us
  waiting for transfers between devices  784 us (82%)
  blocking collectives  89.2 us (9%)
  matrix products  47.9 us (5%)
  between operations  14.3 us (1%)
  other arithmetic  10.6 us (1%)
    reduce_scatter x1, waiting for transfers between devices, body(): lax.psum_scatter(mixed_part.reshape(owners * token_count, width), 'expert...  227 us
    reduce_scatter x1, waiting for transfers between devices, body(): lax.psum_scatter(tokens_part.reshape(owners * token_count, width), 'exper...  226 us
    reduce_scatter x1, waiting for transfers between devices, body(): lax.psum_scatter(gate_part, 'expert', scatter_dimension=0, tiled=True)  179 us
    all_gather x1, waiting for transfers between devices, body(): lax.all_gather(grad_output, 'expert', tiled=True)  69.6 us
    all_gather x1, blocking collectives, body(): lax.all_gather(expert_ids, 'expert', tiled=True).reshape(owners, pair_count)  46.8 us
    reduce_scatter x1, waiting for transfers between devices, body(): lax.psum_scatter(gate_up_local.astype(jnp.bfloat16), 'dp', scatter_dimens...  45.7 us
    all_gather x1, blocking collectives, body(): lax.all_gather(gate_weights, 'expert', tiled=True)  42.4 us
    reduce_scatter x1, waiting for transfers between devices, body(): lax.psum_scatter(down_local.astype(jnp.bfloat16), 'dp', scatter_dimension...  34.5 us
  transfers between devices with their start and end apart: 7, of which 6 were waited for; matrix products, arithmetic and copies ran while one was open for 5% of the time, Pallas kernels for 0%

profile of v1, /device:TPU:2, one launch (start us, length us, event | category | flops | bytes accessed | tf_op | source)
XLA Modules:
  0.0 953.2 jit_solution(4402269293742463482)
XLA Ops:
  7.2 0.7 all-gather.5.cloned.1.call-update
  8.0 0.7 all-gather.7.cloned.1.call-update
  8.7 46.8 %all-gather = s32[32,32,8]{1,2,0:T(8,128)S(1)} all-gather(s32[1,32,8]{1,2,0:T(8,128)} %bitcast.123), channel_id=1, replica_groups=mesh['dp'=8,'expert'=32] {'expert'}, dimensions={0}, use_global_device_ids=true | all-gather | bytes 33792 | tf_op jit(solution)/shard_map/all_gather | solution.py:26
  55.5 0.6 fusion.39
  56.4 0.6 reduce-window.6
  57.3 0.9 copy.20
  58.8 0.8 fusion.30
  59.8 42.4 %all-gather.1 = f32[32,32,8]{1,2,0:T(8,128)S(1)} all-gather(f32[1,32,8]{1,2,0:T(8,128)S(1)} %bitcast.124), channel_id=1, replica_groups=mesh['dp'=8,'expert'=32] {'expert'}, dimensions={0}, use_global_device_ids=true | all-gather | bytes 33792 | tf_op jit(solution)/shard_map/all_gather | solution.py:27
  102.2 0.8 copy.25
  103.0 4.3 convolution_convert_fusion.4
  107.3 69.6 %all-gather.7.cloned.1.call-done = bf16[1024,2048]{1,0:T(8,128)(2,1)} async-done(((bf16[32,2048]{1,0:T(8,128)(2,1)}), bf16[1024,2048]{1,0:T(8,128)(2,1)}) %all-gather.7.cloned.1.call-update) | async-done | bytes 4194320 | tf_op jit(solution)/shard_map/all_gather | solution.py:28
  176.8 3.0 fusion.44
  179.9 7.1 fusion.7
  187.5 3.2 fusion.6
  190.8 1.6 select_reduce_fusion
  192.7 1.1 reshape.312
  193.9 6.0 fusion.20
  200.1 5.5 fusion.33
  205.6 0.9 copy-done.8
  206.7 5.5 fusion
  212.3 2.0 fusion.5
  214.3 3.3 convolution_convert_fusion.2
  217.7 6.7 fusion.17
  224.5 3.4 convolution_convert_fusion.1
  227.9 179.2 %reduce-scatter.10.cloned.1.call-done = f32[32,8]{1,0:T(8,128)} async-done(((f32[1024,8]{1,0:T(8,128)}), f32[32,8]{1,0:T(8,128)}) %reduce-scatter.10.cloned.1.call-update) | async-done | bytes 1040 | tf_op jit(solution)/shard_map/reduce_scatter | solution.py:83
  407.1 1.4 copy.33
  408.4 34.5 %reduce-scatter.14.cloned.1.call-done = bf16[1,768,256]{2,1,0:T(8,128)(2,1)} async-done(((bf16[1,768,2048]{2,1,0:T(8,128)(2,1)}), bf16[1,768,256]{2,1,0:T(8,128)(2,1)}) %reduce-scatter.14.cloned.1.call-update) | async-done | bytes 393232 | tf_op jit(solution)/shard_map/reduce_scatter | solution.py:99
  443.0 1.9 convert_element_type.155
  444.9 45.7 %reduce-scatter.12.cloned.1.call-done = bf16[1,256,1536]{2,1,0:T(8,128)(2,1)} async-done(((bf16[1,2048,1536]{2,1,0:T(8,128)(2,1)}), bf16[1,256,1536]{2,1,0:T(8,128)(2,1)}) %reduce-scatter.12.cloned.1.call-update) | async-done | bytes 786448 | tf_op jit(solution)/shard_map/reduce_scatter | solution.py:96
  490.6 2.5 convert_element_type.152
  493.1 227.1 %reduce-scatter.6.cloned.1.call-done = bf16[32,2048]{1,0:T(8,128)(2,1)} async-done(((bf16[1024,2048]{1,0:T(8,128)(2,1)}), bf16[32,2048]{1,0:T(8,128)(2,1)}) %reduce-scatter.6.cloned.1.call-update) | async-done | bytes 131088 | tf_op jit(solution)/shard_map/reduce_scatter | solution.py:80
  720.2 226.1 %reduce-scatter.8.cloned.1.call-done = bf16[32,2048]{1,0:T(8,128)(2,1)} async-done(((bf16[1024,2048]{1,0:T(8,128)(2,1)}), bf16[32,2048]{1,0:T(8,128)(2,1)}) %reduce-scatter.8.cloned.1.call-update) | async-done | bytes 131088 | tf_op jit(solution)/shard_map/reduce_scatter | solution.py:90
  (46 shorter events, 3.0 us)
Async XLA Ops:
  7.2 180.3 %copy-start = (bf16[1,768,2048]{2,1,0:T(8,128)(2,1)S(1)}, bf16[1,768,2048]{2,1,0:T(8,128)(2,1)}, u32[]{:S(2)}) copy-start(bf16[1,768,2048]{2,1,0:T(8,128)(2,1)} %param.11) | copy-start | bytes 9437188
  7.2 52.6 %copy-start.7 = (f32[32,8]{0,1:T(8,128)S(1)}, f32[32,8]{0,1:T(8,128)}, u32[]{:S(2)}) copy-start(f32[32,8]{0,1:T(8,128)} %param.8) | copy-start | bytes 3076
  7.2 95.8 %all-gather.5.cloned.1.call-start = ((), (), s32[]{:S(2)}) async-start(), calls=%async_computation.5 | async-start | bytes 4325376 | tf_op jit(solution)/shard_map/all_gather | solution.py:25
  7.9 168.9 %all-gather.7.cloned.1.call-start = ((), (), s32[]{:S(2)}) async-start(), calls=%async_computation.7 | async-start | bytes 4325376 | tf_op jit(solution)/shard_map/all_gather | solution.py:28
  8.7 398.4 %reduce-scatter.10.cloned.1.call-start = ((), (), s32[]{:S(2)}) async-start(), calls=%async_computation.9 | async-start | bytes 540672 | tf_op jit(solution)/shard_map/reduce_scatter | solution.py:83
  58.2 0.6 copy-start.6
  176.8 3.0 copy-start.4
  179.9 7.6 copy-start.1
  186.9 3.7 copy-start.2
  187.5 3.2 copy-start.3
  193.8 249.1 %reduce-scatter.14.cloned.1.call-start = ((), (), s32[]{:S(2)}) async-start(), calls=%async_computation.11 | async-start | bytes 3538944 | tf_op jit(solution)/shard_map/reduce_scatter | solution.py:99
  199.8 290.8 %reduce-scatter.12.cloned.1.call-start = ((), (), s32[]{:S(2)}) async-start(), calls=%async_computation.10 | async-start | bytes 7077888 | tf_op jit(solution)/shard_map/reduce_scatter | solution.py:96
  200.1 6.6 copy-start.5
  205.6 0.9 copy-start.8
  205.6 1.1 copy-start.9
  212.3 507.9 %reduce-scatter.6.cloned.1.call-start = ((), (), s32[]{:S(2)}) async-start(), calls=%async_computation.6 | async-start | bytes 4325376 | tf_op jit(solution)/shard_map/reduce_scatter | solution.py:80
  217.7 728.6 %reduce-scatter.8.cloned.1.call-start = ((), (), s32[]{:S(2)}) async-start(), calls=%async_computation.8 | async-start | bytes 4325376 | tf_op jit(solution)/shard_map/reduce_scatter | solution.py:90
Sparse Core Ops, SparseCore 0:
  10.6 84.9 all-gather.4
  98.2 78.5 all-gather.6
  193.9 213.0 reduce-scatter.9
  409.5 33.4 reduce-scatter.13
  445.4 45.2 reduce-scatter.11
  494.9 225.2 reduce-scatter.5
  724.7 221.5 reduce-scatter.7
